TPU v7x, 32 devices: a whole 2x2x4 slice. The times are simulated.
32 devices in a mesh: seq: 8 (over y, x, core), chan: 4 (over z).
Axes of the slice: x: 2, y: 2, z: 4, core: 2. Of those that a mesh axis runs over, the one named last changes fastest.
Arguments:
- query_proj: bfloat16 [1024, 8192], P('seq', 'chan'), may hold values from -8 to 8
- key_proj: bfloat16 [1024, 8192], P('seq', 'chan'), may hold values from -8 to 8
- value_proj: bfloat16 [1024, 8192], P('seq', 'chan'), may hold values from -6 to 6
- residual: bfloat16 [1024, 8192], P('seq', 'chan'), may hold values from -6 to 6
- out_weight: bfloat16 [8192, 8192], P('chan', 'seq'), may hold values from -0.0625 to 0.0625
Outputs:
- attn_out: bfloat16 [1024, 8192], P('seq', 'chan')
All inputs are finite; a program needn't handle non-finite values.
Results may differ from a plain program's by a relative error of at most 0.008.
Values may be sent and summed in bfloat16 or wider, within the bound.
No kernel may reach another device: no remote copies, remote signals or barrier semaphores. Data moves between devices by JAX's collectives and lax.ppermute only.
A program may use at most 64 MiB of HBM per device.

v0:
```python
import math
import jax
import jax.numpy as jnp
from jax import lax
from jax.sharding import PartitionSpec as P

HEAD_DIM = 128


def attend(state, query_rows, first_pos, key_block, value_block, block_start, score_scale):
    row_max, row_total, accum = state
    scores = (
        jnp.einsum("qhd,khd->hqk", query_rows, key_block, preferred_element_type=jnp.float32)
        * score_scale
    )
    row_pos = first_pos + jnp.arange(query_rows.shape[0], dtype=jnp.int32)
    col_pos = block_start + jnp.arange(key_block.shape[0], dtype=jnp.int32)
    allowed = (col_pos[None, :] <= row_pos[:, None])[None]
    scores = jnp.where(allowed, scores, -1e30)
    new_max = jnp.maximum(row_max, jnp.max(scores, axis=-1))
    weights = jnp.where(allowed, jnp.exp(scores - new_max[..., None]), 0.0)
    factor = jnp.exp(row_max - new_max)
    row_total = row_total * factor + jnp.sum(weights, axis=-1)
    accum = accum * factor[..., None] + jnp.einsum(
        "hqk,khd->hqd",
        weights.astype(jnp.bfloat16),
        value_block,
        preferred_element_type=jnp.float32,
    )
    return (new_max, row_total, accum)


def guarded(state, query_rows, first_pos, key_block, value_block, block_start, score_scale):
    last_pos = first_pos + query_rows.shape[0] - 1

    def do_update(inner):
        return attend(
            inner, query_rows, first_pos, key_block, value_block, block_start, score_scale
        )

    def keep_state(inner):
        return inner

    return lax.cond(block_start <= last_pos, do_update, keep_state, state)


def per_device(query_proj, key_proj, value_proj, residual, out_weight):
    seg_rows = query_proj.shape[0]
    feat_width = query_proj.shape[1]
    heads_here = feat_width // HEAD_DIM
    seq_count = lax.axis_size("seq")
    chan_count = lax.axis_size("chan")
    segment = lax.axis_index("seq")
    score_scale = 1.0 / math.sqrt(HEAD_DIM)
    groups = [(query_proj, segment * seg_rows)]
    shaped = [
        (rows.reshape(rows.shape[0], heads_here, HEAD_DIM), first_pos) for rows, first_pos in groups
    ]
    starting = tuple(
        (
            (
                jnp.full((heads_here, rows.shape[0]), -1e30, jnp.float32),
                jnp.zeros((heads_here, rows.shape[0]), jnp.float32),
                jnp.zeros((heads_here, rows.shape[0], HEAD_DIM), jnp.float32),
            )
            for rows, first_pos in shaped
        )
    )
    piece_keys = lax.all_gather(key_proj, "seq", axis=0, tiled=True)
    piece_values = lax.all_gather(value_proj, "seq", axis=0, tiled=True)
    piece_rows = piece_keys.shape[0]

    def one_block(block_index, states):
        offset = block_index * seg_rows
        key_block = lax.dynamic_slice_in_dim(piece_keys, offset, seg_rows, 0).reshape(
            seg_rows, heads_here, HEAD_DIM
        )
        value_block = lax.dynamic_slice_in_dim(piece_values, offset, seg_rows, 0).reshape(
            seg_rows, heads_here, HEAD_DIM
        )
        updated = []
        for (query_rows, first_pos), state in zip(shaped, states):
            updated.append(
                guarded(state, query_rows, first_pos, key_block, value_block, offset, score_scale)
            )
        return tuple(updated)

    finals = lax.fori_loop(0, piece_rows // seg_rows, one_block, starting)
    pieces_out = []
    for row_max, row_total, accum in finals:
        ratio = accum / row_total[..., None]
        pieces_out.append(
            ratio.transpose(1, 0, 2).reshape(ratio.shape[1], feat_width).astype(jnp.bfloat16)
        )
    local_context = pieces_out[0]
    gathered = lax.all_gather(local_context, "seq", axis=0, tiled=True)
    sub_rows = seg_rows // chan_count
    grid = gathered.reshape(seq_count, chan_count, sub_rows, feat_width)
    block_tokens = seq_count * sub_rows
    rows = grid.transpose(1, 0, 2, 3).reshape(block_tokens * lax.axis_size("chan"), feat_width)
    partial_sums = lax.psum_scatter(
        jnp.dot(rows, out_weight, preferred_element_type=jnp.float32).astype(jnp.bfloat16),
        "chan",
        scatter_dimension=0,
        tiled=True,
    ).astype(jnp.float32)
    relaid = lax.all_to_all(
        lax.all_to_all(
            partial_sums.astype(jnp.bfloat16), "seq", split_axis=0, concat_axis=1, tiled=True
        ),
        "chan",
        split_axis=1,
        concat_axis=0,
        tiled=True,
    ).astype(partial_sums.dtype)
    return (residual.astype(jnp.float32) + relaid).astype(jnp.bfloat16)


def solution(mesh):
    placed = (
        P("seq", "chan"),
        P("seq", "chan"),
        P("seq", "chan"),
        P("seq", "chan"),
        P("chan", "seq"),
    )
    return jax.shard_map(
        per_device, mesh=mesh, in_specs=placed, out_specs=P("seq", "chan"), check_vma=False
    )
```

profile of v0, /device:TPU:0, one launch (start us, length us, event | category | flops | bytes accessed | tf_op | source)
XLA Modules:
  0.0 250.2 jit_solution(13693621716920695424)
XLA Ops:
  6.5 0.0 all-gather.4.cloned.1.call-start
  6.5 2.0 copy.32
  8.6 0.0 all-gather.4.cloned.1.call-update
  8.6 0.0 all-gather.6.cloned.1.call-start
  8.7 2.1 copy.34
  10.7 0.0 all-gather.6.cloned.1.call-update
  10.8 0.0 all-gather.8.cloned.1.call-start
  10.8 1.3 copy.33
  12.1 0.3 copy.35
  12.4 37.0 %all-gather.4.cloned.1.call-done = bf16[1024,2048]{0,1:T(8,128)(2,1)} async-done(((bf16[128,2048]{0,1:T(8,128)(2,1)}), bf16[1024,2048]{0,1:T(8,128)(2,1)}) %all-gather.4.cloned.1.call-update) | async-done | bytes 4194320 | tf_op jit(solution)/shard_map/all_gather | solution.py:69
  49.4 39.3 %all-gather.6.cloned.1.call-done = bf16[1024,2048]{0,1:T(8,128)(2,1)} async-done(((bf16[128,2048]{0,1:T(8,128)(2,1)}), bf16[1024,2048]{0,1:T(8,128)(2,1)}) %all-gather.6.cloned.1.call-update) | async-done | bytes 4194320 | tf_op jit(solution)/shard_map/all_gather | solution.py:70
  88.8 0.1 broadcast_in_dim.45
  88.9 3.3 %while.19 = (s32[]{:T(128)}, f32[16,128]{1,0:T(8,128)S(1)}, f32[16,128]{1,0:T(8,128)S(1)}, f32[16,128,128]{2,1,0:T(8,128)S(1)}, s32[]{:T(128)}, /*index=5*/s32[]...) while((s32[]{:T(128)}, f32[16,128]{1,0:T(8,128)S(1)}, ...), condition=%wide.region_5.6_spmd, body=%wide.region_0.5_spmd.sunk | while | flops 137122048 | bytes 9111853 | solution.py:88
  88.9 3.0 %conditional.2 = ((f32[16,128]{1,0:T(8,128)S(1)}, f32[16,128]{1,0:T(8,128)S(1)}, f32[16,128,128]{2,1,0:T(8,128)S(1)})) conditional(s32[]{:T(128)} %convert_element_type.63, (f32[16,128]{1,0:T(8,128)S(1)}, f32[16,128]{1,0:T(8,128)S(1)}, f32[16,128,128]{2,1,0:T(8,128)S(1)}) %tuple.61, (s32[]{:T(128)}, s32[]{:T(128)}, bf16[1024,2048]{0,1:T(8,128)(2,1)}, ...), branch_computations={%region_1.0_spmd, %region_2.4_spmd} | conditional | flops 137122048 | bytes 9111630 | solution.py:44
  88.9 1.3 constant_dynamic-slice_fusion
  90.2 0.1 broadcast_compare_fusion
  90.3 0.5 fusion.10
  90.8 0.2 fusion.3
  91.1 0.8 convolution_add_fusion
  92.2 0.3 copy.36
  92.5 0.9 divide_convert_fusion
  93.5 0.0 all-gather.8.cloned.1.call-update
  93.5 0.0 reduce-scatter.2.cloned.1.call-start
  93.5 58.4 %all-gather.8.cloned.1.call-done = bf16[1024,2048]{0,1:T(8,128)(2,1)} async-done(((bf16[128,2048]{0,1:T(8,128)(2,1)}), bf16[1024,2048]{0,1:T(8,128)(2,1)}) %all-gather.8.cloned.1.call-update) | async-done | bytes 4194320 | tf_op jit(solution)/shard_map/all_gather | solution.py:96
  151.9 6.5 %copy.37 = bf16[1024,2048]{1,0:T(8,128)(2,1)} copy(bf16[1024,2048]{0,1:T(8,128)(2,1)} %all-gather.8.cloned.1.call-done) | data formatting | bytes 8388608 | tf_op jit(solution)/shard_map/all_gather | solution.py:96
  158.4 0.0 copy-start.1
  158.4 2.7 %copy.38 = bf16[4,8,32,2048]{3,2,1,0:T(8,128)(2,1)S(1)} copy(bf16[4,8,32,2048]{3,2,0,1:T(8,128)(2,1)} %bitcast.29) | data formatting | bytes 8388608 | tf_op jit(solution)/shard_map/transpose | solution.py:100
  161.1 0.8 copy-done.1
  161.9 5.7 %convolution_convert_fusion = bf16[1024,1024]{1,0:T(8,128)(2,1)} fusion(bf16[1024,2048]{1,0:T(8,128)(2,1)S(1)} %bitcast.30, bf16[2048,1024]{1,0:T(8,128)(2,1)S(1)} %copy-done.1), kind=kOutput, calls=%fused_computation.18 | convolution fusion | flops 4296015872 | bytes 10485760 | tf_op jit(solution)/shard_map/dot_general | solution.py:102
  167.6 0.0 copy-start
  167.6 0.0 reduce-scatter.2.cloned.1.call-update
  167.7 44.0 %reduce-scatter.2.cloned.1.call-done = bf16[256,1024]{1,0:T(8,128)(2,1)} async-done(((bf16[1024,1024]{1,0:T(8,128)(2,1)}), bf16[256,1024]{1,0:T(8,128)(2,1)}) %reduce-scatter.2.cloned.1.call-update) | async-done | bytes 524304 | tf_op jit(solution)/shard_map/reduce_scatter | solution.py:101
  211.7 13.4 %all_to_all.29 = bf16[8,32,1024]{2,1,0:T(8,128)(2,1)S(1)} all-to-all(bf16[8,32,1024]{2,1,0:T(8,128)(2,1)} %bitcast.34), channel_id=1, replica_groups=mesh['seq'=8,'chan'=4] {'seq'}, dimensions={0} | all-to-all | bytes 1048576 | tf_op jit(solution)/shard_map/all_to_all | solution.py:108
  225.1 0.3 copy.39
  225.3 0.4 all_to_all.25
  225.7 0.3 copy.40
  226.0 16.7 %all_to_all.30 = bf16[32,4,2048]{2,0,1:T(8,128)(2,1)S(1)} all-to-all(bf16[32,4,2048]{2,0,1:T(8,128)(2,1)S(1)} %copy.40), channel_id=1, replica_groups=mesh['seq'=8,'chan'=4] {'chan'}, dimensions={1} | all-to-all | bytes 1048576 | tf_op jit(solution)/shard_map/all_to_all | solution.py:107
  242.7 0.0 copy-done
  242.7 0.9 fusion.9
  (13 shorter events, 0.1 us)
Async XLA Ops:
  6.5 42.9 %all-gather.4.cloned.1.call-start = ((), (), s32[]{:S(2)}) async-start(), calls=%async_computation.3 | async-start | bytes 4718592 | tf_op jit(solution)/shard_map/all_gather | solution.py:69
  8.6 80.1 %all-gather.6.cloned.1.call-start = ((), (), s32[]{:S(2)}) async-start(), calls=%async_computation.4 | async-start | bytes 4718592 | tf_op jit(solution)/shard_map/all_gather | solution.py:70
  10.8 141.2 %all-gather.8.cloned.1.call-start = ((), (), s32[]{:S(2)}) async-start(), calls=%async_computation.5 | async-start | bytes 4718592 | tf_op jit(solution)/shard_map/all_gather | solution.py:96
  93.5 118.2 %reduce-scatter.2.cloned.1.call-start = ((), (), s32[]{:S(2)}) async-start(), calls=%async_computation.6 | async-start | bytes 2621440 | tf_op jit(solution)/shard_map/reduce_scatter | solution.py:101
  158.4 3.4 %copy-start.1 = (bf16[2048,1024]{1,0:T(8,128)(2,1)S(1)}, bf16[2048,1024]{1,0:T(8,128)(2,1)}, u32[]{:S(2)}) copy-start(bf16[2048,1024]{1,0:T(8,128)(2,1)} %param.13) | copy-start | bytes 12582916
  167.6 75.1 %copy-start = (bf16[128,2048]{1,0:T(8,128)(2,1)S(1)}, bf16[128,2048]{1,0:T(8,128)(2,1)}, u32[]{:S(2)}) copy-start(bf16[128,2048]{1,0:T(8,128)(2,1)} %param.12) | copy-start | bytes 1572868
Sparse Core Ops, SparseCore 0:
  9.2 40.1 all-gather.3
  51.3 37.4 all-gather.5
  93.6 58.2 all-gather.7
  167.8 43.8 reduce-scatter.1
where the time goes:
time: 251 us; the launch traced here: 250 us
  waiting for transfers between devices  179 us (71%)
  blocking collectives  30.1 us (12%)
  local copies, waits for them, and re-layouts  18.4 us (7%)
  between operations  13.2 us (5%)
  matrix products  7.06 us (3%)
    all_gather x1, waiting for transfers between devices, per_device(): gathered = lax.all_gather(local_context, 'seq', axis=0, tiled=True)  58.4 us
    reduce_scatter x1, waiting for transfers between devices, per_device(): lax.psum_scatter(jnp.dot(rows, out_weight, preferred_element_type=jnp.flo...  44 us
    all_gather x1, waiting for transfers between devices, per_device(): piece_values = lax.all_gather(value_proj, 'seq', axis=0, tiled=True)  39.3 us
    all_gather x1, waiting for transfers between devices, per_device(): piece_keys = lax.all_gather(key_proj, 'seq', axis=0, tiled=True)  37 us
    all_to_all x1, blocking collectives, per_device(): lax.all_to_all(lax.all_to_all(partial_sums.astype(jnp.bfloat16), 'seq', s...  16.7 us
    all_to_all x1, blocking collectives, per_device(): lax.all_to_all(partial_sums.astype(jnp.bfloat16), 'seq', split_axis=0, co...  13.4 us
    all_gather x1, local copies, waits for them, and re-layouts, per_device(): gathered = lax.all_gather(local_context, 'seq', axis=0, tiled=True)  6.53 us
    unnamed x7, local copies, waits for them, and re-layouts  6.22 us
  transfers between devices with their start and end apart: 4, of which 4 were waited for; matrix products, arithmetic and copies ran while one was open for 1% of the time, Pallas kernels for 0%

commit v1 on v0

--- a/solution.py
+++ b/solution.py
@@ -66,8 +66,11 @@
             for rows, first_pos in shaped
         )
     )
-    piece_keys = lax.all_gather(key_proj, "seq", axis=0, tiled=True)
-    piece_values = lax.all_gather(value_proj, "seq", axis=0, tiled=True)
+    piece_keys, piece_values = jnp.split(
+        lax.all_gather(jnp.concatenate([key_proj, value_proj], axis=1), "seq", axis=0, tiled=True),
+        [key_proj.shape[1]],
+        axis=1,
+    )
     piece_rows = piece_keys.shape[0]
 
     def one_block(block_index, states):

time: 251 us -> 237 us (0.944)
  waiting for transfers between devices: 179 us -> 161 us
  local copies, waits for them, and re-layouts: 18.4 us -> 21.8 us
    all_gather x2 -> x1, waiting for transfers between devices: 76.3 us -> 58.2 us  [per_device(): lax.all_gather(jnp.concatenate([key_proj, value_proj], axis=1), 'seq', ax...]
    split x0 -> x1, local copies, waits for them, and re-layouts: none -> 5.9 us  [per_device(): jnp.split(lax.all_gather(jnp.concatenate([key_proj, value_proj], axis=1),...]
    unnamed x7 -> x9, local copies, waits for them, and re-layouts: 6.22 us -> 3.74 us
  transfers between devices with their start and end apart: 4 -> 3, of which waited for: 4 -> 3; matrix products, arithmetic and copies ran while one was open for 1% -> 0% of each run, Pallas kernels for 0% -> 0%
where the time goes in v1:
time: 237 us
  waiting for transfers between devices  161 us (68%)
  blocking collectives  30 us (13%)
  local copies, waits for them, and re-layouts  21.8 us (9%)
  between operations  13.2 us (6%)
  matrix products  7.06 us (3%)
  other arithmetic  3.28 us (1%)
    all_gather x1, waiting for transfers between devices, per_device(): gathered = lax.all_gather(local_context, 'seq', axis=0, tiled=True)  58.4 us
    all_gather x1, waiting for transfers between devices, per_device(): lax.all_gather(jnp.concatenate([key_proj, value_proj], axis=1), 'seq', ax...  58.2 us
    reduce_scatter x1, waiting for transfers between devices, per_device(): lax.psum_scatter(jnp.dot(rows, out_weight, preferred_element_type=jnp.flo...  44 us
    all_to_all x1, blocking collectives, per_device(): lax.all_to_all(lax.all_to_all(partial_sums.astype(jnp.bfloat16), 'seq', s...  16.7 us
    all_to_all x1, blocking collectives, per_device(): lax.all_to_all(partial_sums.astype(jnp.bfloat16), 'seq', split_axis=0, co...  13.4 us
    all_gather x1, local copies, waits for them, and re-layouts, per_device(): gathered = lax.all_gather(local_context, 'seq', axis=0, tiled=True)  6.53 us
    split x1, local copies, waits for them, and re-layouts, per_device(): jnp.split(lax.all_gather(jnp.concatenate([key_proj, value_proj], axis=1),...  5.9 us
    dot_general x1, matrix products, per_device(): jnp.dot(rows, out_weight, preferred_element_type=jnp.float32)  5.73 us
  transfers between devices with their start and end apart: 3, of which 3 were waited for; matrix products, arithmetic and copies ran while one was open for 0% of the time, Pallas kernels for 0%

profile of v1, /device:TPU:0, one launch (start us, length us, event | category | flops | bytes accessed | tf_op | source)
XLA Modules:
  0.0 236.5 jit_solution(5387086142434809409)
XLA Ops:
  6.5 0.0 copy-start.1
  6.5 0.0 all-gather.3.cloned.1.call-start
  6.5 1.4 copy.32
  7.9 1.3 copy.33
  9.2 1.1 pad_maximum_fusion
  10.4 0.0 all-gather.3.cloned.1.call-update
  10.4 0.0 all-gather.5.cloned.1.call-start
  10.4 0.0 copy-done.1
  10.5 0.3 copy.34
  10.7 0.3 copy.35
  11.0 58.2 %all-gather.3.cloned.1.call-done = bf16[1024,4096]{0,1:T(8,128)(2,1)} async-done(((bf16[128,4096]{0,1:T(8,128)(2,1)}), bf16[1024,4096]{0,1:T(8,128)(2,1)}) %all-gather.3.cloned.1.call-update) | async-done | bytes 8388624 | tf_op jit(solution)/shard_map/all_gather | solution.py:70
  69.2 5.9 %fusion.11 = (bf16[1024,2048]{0,1:T(8,128)(2,1)}, bf16[1024,2048]{0,1:T(8,128)(2,1)}) fusion(bf16[1024,4096]{0,1:T(8,128)(2,1)} %all-gather.3.cloned.1.call-done), kind=kLoop, calls=%fused_computation.24 | loop fusion | bytes 16777216 | tf_op jit(solution)/shard_map/split | solution.py:69
  75.1 0.1 broadcast_in_dim.45
  75.2 3.3 %while.19 = (s32[]{:T(128)}, f32[16,128]{1,0:T(8,128)S(1)}, f32[16,128]{1,0:T(8,128)S(1)}, f32[16,128,128]{2,1,0:T(8,128)S(1)}, s32[]{:T(128)}, /*index=5*/s32[]...) while((s32[]{:T(128)}, f32[16,128]{1,0:T(8,128)S(1)}, ...), condition=%wide.region_5.6_spmd, body=%wide.region_0.5_spmd.sunk | while | flops 137122048 | bytes 9111853 | solution.py:91
  75.2 3.0 %conditional.2 = ((f32[16,128]{1,0:T(8,128)S(1)}, f32[16,128]{1,0:T(8,128)S(1)}, f32[16,128,128]{2,1,0:T(8,128)S(1)})) conditional(s32[]{:T(128)} %convert_element_type.63, (f32[16,128]{1,0:T(8,128)S(1)}, f32[16,128]{1,0:T(8,128)S(1)}, f32[16,128,128]{2,1,0:T(8,128)S(1)}) %tuple.62, (s32[]{:T(128)}, s32[]{:T(128)}, bf16[1024,2048]{0,1:T(8,128)(2,1)}, ...), branch_computations={%region_1.0_spmd, %region_2.4_spmd} | conditional | flops 137122048 | bytes 9111630 | solution.py:44
  75.3 1.3 constant_dynamic-slice_fusion
  76.6 0.1 broadcast_compare_fusion
  76.7 0.5 fusion.10
  77.2 0.2 fusion.3
  77.4 0.8 convolution_add_fusion
  78.6 0.3 copy.36
  78.9 0.9 divide_convert_fusion
  79.8 0.0 all-gather.5.cloned.1.call-update
  79.9 0.0 reduce-scatter.2.cloned.1.call-start
  79.9 58.4 %all-gather.5.cloned.1.call-done = bf16[1024,2048]{0,1:T(8,128)(2,1)} async-done(((bf16[128,2048]{0,1:T(8,128)(2,1)}), bf16[1024,2048]{0,1:T(8,128)(2,1)}) %all-gather.5.cloned.1.call-update) | async-done | bytes 4194320 | tf_op jit(solution)/shard_map/all_gather | solution.py:99
  138.3 6.5 %copy.37 = bf16[1024,2048]{1,0:T(8,128)(2,1)} copy(bf16[1024,2048]{0,1:T(8,128)(2,1)} %all-gather.5.cloned.1.call-done) | data formatting | bytes 8388608 | tf_op jit(solution)/shard_map/all_gather | solution.py:99
  144.8 0.0 copy-start.2
  144.8 2.7 %copy.38 = bf16[4,8,32,2048]{3,2,1,0:T(8,128)(2,1)S(1)} copy(bf16[4,8,32,2048]{3,2,0,1:T(8,128)(2,1)} %bitcast.29) | data formatting | bytes 8388608 | tf_op jit(solution)/shard_map/transpose | solution.py:103
  147.5 0.8 copy-done.2
  148.3 5.7 %convolution_convert_fusion = bf16[1024,1024]{1,0:T(8,128)(2,1)} fusion(bf16[1024,2048]{1,0:T(8,128)(2,1)S(1)} %bitcast.30, bf16[2048,1024]{1,0:T(8,128)(2,1)S(1)} %copy-done.2), kind=kOutput, calls=%fused_computation.18 | convolution fusion | flops 4296015872 | bytes 10485760 | tf_op jit(solution)/shard_map/dot_general | solution.py:105
  154.0 0.0 copy-start
  154.0 0.0 reduce-scatter.2.cloned.1.call-update
  154.0 44.0 %reduce-scatter.2.cloned.1.call-done = bf16[256,1024]{1,0:T(8,128)(2,1)} async-done(((bf16[1024,1024]{1,0:T(8,128)(2,1)}), bf16[256,1024]{1,0:T(8,128)(2,1)}) %reduce-scatter.2.cloned.1.call-update) | async-done | bytes 524304 | tf_op jit(solution)/shard_map/reduce_scatter | solution.py:104
  198.1 13.4 %all_to_all.29 = bf16[8,32,1024]{2,1,0:T(8,128)(2,1)S(1)} all-to-all(bf16[8,32,1024]{2,1,0:T(8,128)(2,1)} %bitcast.34), channel_id=1, replica_groups=mesh['seq'=8,'chan'=4] {'seq'}, dimensions={0} | all-to-all | bytes 1048576 | tf_op jit(solution)/shard_map/all_to_all | solution.py:111
  211.4 0.3 copy.39
  211.7 0.4 all_to_all.25
  212.1 0.3 copy.40
  212.4 16.7 %all_to_all.30 = bf16[32,4,2048]{2,0,1:T(8,128)(2,1)S(1)} all-to-all(bf16[32,4,2048]{2,0,1:T(8,128)(2,1)S(1)} %copy.40), channel_id=1, replica_groups=mesh['seq'=8,'chan'=4] {'chan'}, dimensions={1} | all-to-all | bytes 1048576 | tf_op jit(solution)/shard_map/all_to_all | solution.py:110
  229.1 0.0 copy-done
  229.1 0.9 fusion.9
  (13 shorter events, 0.1 us)
Async XLA Ops:
  6.5 3.9 %copy-start.1 = (bf16[128,2048]{1,0:T(8,128)(2,1)S(1)}, bf16[128,2048]{1,0:T(8,128)(2,1)}, u32[]{:S(2)}) copy-start(bf16[128,2048]{1,0:T(8,128)(2,1)} %param.9) | copy-start | bytes 1572868
  6.5 62.7 %all-gather.3.cloned.1.call-start = ((), (), s32[]{:S(2)}) async-start(), calls=%async_computation.3 | async-start | bytes 9437184 | tf_op jit(solution)/shard_map/all_gather | solution.py:70
  10.4 127.9 %all-gather.5.cloned.1.call-start = ((), (), s32[]{:S(2)}) async-start(), calls=%async_computation.4 | async-start | bytes 4718592 | tf_op jit(solution)/shard_map/all_gather | solution.py:99
  79.9 118.2 %reduce-scatter.2.cloned.1.call-start = ((), (), s32[]{:S(2)}) async-start(), calls=%async_computation.5 | async-start | bytes 2621440 | tf_op jit(solution)/shard_map/reduce_scatter | solution.py:104
  144.8 3.4 %copy-start.2 = (bf16[2048,1024]{1,0:T(8,128)(2,1)S(1)}, bf16[2048,1024]{1,0:T(8,128)(2,1)}, u32[]{:S(2)}) copy-start(bf16[2048,1024]{1,0:T(8,128)(2,1)} %param.13) | copy-start | bytes 12582916
  154.0 75.1 %copy-start = (bf16[128,2048]{1,0:T(8,128)(2,1)S(1)}, bf16[128,2048]{1,0:T(8,128)(2,1)}, u32[]{:S(2)}) copy-start(bf16[128,2048]{1,0:T(8,128)(2,1)} %param.12) | copy-start | bytes 1572868
Sparse Core Ops, SparseCore 0:
  10.5 58.6 all-gather.2
  80.0 58.2 all-gather.4
  154.1 43.8 reduce-scatter.1
